TPU v7x, 128 devices: a whole 4x4x4 slice. The times are simulated.
128 devices in a mesh: fsdp: 32 (over z, y, core), fac: 4 (over x).
Axes of the slice: x: 4, y: 4, z: 4, core: 2. Of those that a mesh axis runs over, the one named last changes fastest.
Arguments:
- activations: bfloat16 [32768, 3072], P('fsdp'), may hold values from -6 to 6
- out_grads: bfloat16 [32768, 3072], P('fsdp', 'fac'), may hold values from -12 to 12
- token_ids: int32 [32768], P('fsdp'), may hold values from 0 to 32767
- forget_mask: int32 [32768], P('fsdp'), may hold values 0 or 1
- importance: float32 [32768], replicated, may hold values from 0.3 to 3
- in_inverse: bfloat16 [3072, 3072], P('fsdp'), may hold values from -1 to 3, as said below
- out_inverse: bfloat16 [3072, 3072], P(None, 'fac'), may hold values from -1 to 3, as said below
Outputs:
- newton_step: float32 [3072, 3072], P('fsdp', 'fac')
- residual: float32 [3072, 3072], P('fsdp', 'fac')
Inputs may be any that keep to these rules, and one draw needn't show every extreme that they name: `in_inverse`: symmetric and positive definite. `out_inverse`: symmetric and positive definite.
All inputs are finite; a program needn't handle non-finite values. No bound on the sum of `forget_mask` on one device may be relied on, other than what follows from the above.
Results may differ from a plain program's by a relative error of at most 0.03.
Values may be sent and summed in bfloat16 or wider, within the bound.
No kernel may reach another device: no remote copies, remote signals or barrier semaphores. Data moves between devices by JAX's collectives and lax.ppermute only.
A program may use at most 64 MiB of HBM per device.

v0:
```python
import math
import jax
import jax.numpy as jnp
from jax import lax
from jax.sharding import PartitionSpec as P

ITERS = 2
damping = 0.3


def add_columns(matrix, piece):
    return jnp.dot(matrix, piece, preferred_element_type=jnp.float32)


def transposed_term(matrix, right):
    return lax.dot_general(
        matrix, right, (((0,), (0,)), ((), ())), preferred_element_type=jnp.float32
    )


FSDP = ("pairs", "core")


def ring_product(piece, right):
    n = lax.axis_size("fac")
    me = lax.axis_index("fac")
    width = piece.shape[1]

    def right_block(k):
        return lax.dynamic_slice_in_dim(right, k % n * width, width, axis=0)

    total = add_columns(piece, right_block(me))
    ahead = piece
    behind = piece
    for step in range(1, n // 2 + 1):
        ahead = lax.ppermute(ahead, "fac", [(j, (j + 1) % n) for j in range(n)])
        total = total + add_columns(ahead, right_block(me - step))
        if 2 * step < n:
            behind = lax.ppermute(behind, "fac", [(j, (j - 1) % n) for j in range(n)])
            total = total + add_columns(behind, right_block(me + step))
    return total


def scatter_sum(partial):
    pairs, cores = (lax.axis_size("pairs"), lax.axis_size("core"))
    blocks = partial.reshape(pairs, cores, partial.shape[0] // (pairs * cores), partial.shape[1])
    on_chip = lax.all_to_all(blocks, "core", 1, 1, tiled=False)
    chip_sum = jnp.sum(on_chip.astype(jnp.float32), axis=1).astype(jnp.bfloat16)
    received = lax.all_to_all(chip_sum, "pairs", 0, 0, tiled=False)
    return lax.optimization_barrier(jnp.sum(received.astype(jnp.float32), axis=0))


def global_sums(*partials):
    devices = lax.axis_size("pairs") * lax.axis_size("core") * lax.axis_size("fac")
    stacked = jnp.broadcast_to(jnp.stack(partials)[None, :], (devices, len(partials)))
    received = lax.all_to_all(stacked, FSDP + ("fac",), 0, 0, tiled=True)
    total = jnp.sum(received, axis=0)
    return tuple((total[i] for i in range(len(partials))))


def body(activations, out_grads, token_ids, forget_mask, importance, in_inverse, out_inverse):
    tok_rows, d_in = activations.shape
    total = tok_rows * lax.axis_size("pairs") * lax.axis_size("core")
    keep = 1.0 - forget_mask.astype(jnp.float32)
    weights = importance[token_ids] * keep / total
    forget_grads = out_grads * forget_mask.astype(jnp.bfloat16)[:, None]
    grad_scale = 1.0 / math.sqrt(total)
    gradient = scatter_sum(
        (transposed_term(activations, forget_grads) * grad_scale).astype(jnp.bfloat16)
    )

    def gather_rows(matrix):
        return lax.all_gather(matrix.astype(jnp.bfloat16), FSDP, axis=0, tiled=True)

    def precondition(gathered):
        mixed = add_columns(in_inverse, gathered)
        mixed_low = mixed.astype(jnp.bfloat16)
        return jnp.dot(
            lax.all_gather(mixed_low, "fac", axis=1, tiled=True),
            out_inverse,
            preferred_element_type=jnp.float32,
        )

    def inner_part(left, right):
        return jnp.sum(left * right)

    d_out_part = out_inverse.shape[1]
    in_cols = lax.all_gather(
        lax.dynamic_slice_in_dim(
            in_inverse, lax.axis_index("fac") * d_out_part, d_out_part, axis=1
        ),
        FSDP,
        axis=0,
        tiled=True,
    )
    gradient, in_cols = lax.optimization_barrier((gradient, in_cols))
    residual = -gradient
    residual_rows = gather_rows(residual)
    gram_cols = d_in // lax.axis_size("fac")
    own_cols = lax.dynamic_slice_in_dim(
        activations, lax.axis_index("fac") * gram_cols, gram_cols, axis=1
    )
    weighted = (own_cols * weights[:, None]).astype(jnp.bfloat16)
    half = gram_cols // 2
    gram_first = transposed_term(activations, weighted[:, :half]).astype(jnp.bfloat16)
    gram_second = transposed_term(activations, weighted[:, half:]).astype(jnp.bfloat16)
    residual_rows, first_rows = lax.optimization_barrier((residual_rows, scatter_sum(gram_first)))
    precond = precondition(residual_rows)
    gram_own = jnp.concatenate([first_rows, scatter_sum(gram_second)], axis=1)
    gram_rows = lax.all_gather(gram_own.astype(jnp.bfloat16), "fac", axis=1, tiled=True)

    def curvature(matrix):
        return add_columns(gram_rows, gather_rows(matrix)) + damping * matrix

    direction = precond
    image = curvature(direction)
    image_rows = gather_rows(image)
    inner_now, energy = global_sums(inner_part(residual, precond), inner_part(direction, image))
    gram_inverse = lax.all_gather(
        add_columns(gram_rows, in_cols).astype(jnp.bfloat16), "fac", axis=1, tiled=True
    )
    alpha = inner_now / energy
    newton_step = alpha * direction
    residual = residual - alpha * image
    next_rows = (residual_rows.astype(jnp.float32) - alpha * image_rows.astype(jnp.float32)).astype(
        jnp.bfloat16
    )
    rows = in_inverse.shape[0]
    left = jnp.concatenate([in_inverse, gram_inverse], axis=0)
    both = add_columns(left, next_rows).astype(jnp.bfloat16)
    both_out = ring_product(both, out_inverse)
    precond = both_out[:rows]
    precond_image = both_out[rows:] + damping * precond
    inner_next, z_hz, z_hd, d_hz = global_sums(
        inner_part(residual, precond),
        inner_part(precond, precond_image),
        inner_part(precond, image),
        inner_part(direction, precond_image),
    )
    beta = inner_next / inner_now
    direction = precond + beta * direction
    image = precond_image + beta * image
    energy = z_hz + beta * (z_hd + d_hz) + beta * beta * energy
    alpha = inner_next / energy
    newton_step = newton_step + alpha * direction
    residual = residual - alpha * image
    return (newton_step, residual)


def solution(mesh):
    cores = 2
    split = jax.sharding.Mesh(
        mesh.devices.reshape(mesh.shape["fsdp"] // cores, cores, mesh.shape["fac"]),
        ("pairs", "core", "fac"),
    )
    placed = (P(FSDP, None), P(FSDP, "fac"), P(FSDP), P(FSDP), P(), P(FSDP, None), P(None, "fac"))
    return jax.shard_map(
        body,
        mesh=split,
        in_specs=placed,
        out_specs=(P(FSDP, "fac"), P(FSDP, "fac")),
        check_vma=False,
    )
```

profile of v0, /device:TPU:1, one launch (start us, length us, event | category | flops | bytes accessed | tf_op | source)
XLA Modules:
  0.0 333.9 jit_solution(15328082240654221681)
XLA Ops:
  7.2 0.0 all-gather.5.cloned.1.call-start
  7.2 1.6 constant_dynamic-slice_fusion
  8.8 0.0 all-gather.5.cloned.1.call-update
  8.8 0.0 all-gather.7.cloned.1.call-start
  8.9 0.7 convert_element_type.76
  9.6 9.4 %fusion.2 = bf16[3072,768]{0,1:T(8,128)(2,1)} fusion(bf16[1024,3072]{1,0:T(8,128)(2,1)} %param.7, bf16[1024,768]{1,0:T(8,128)(2,1)} %param.8, bf16[1024]{0:T(1024)(128)(2,1)S(1)} %convert_element_type.76), kind=kOutput, calls=%fused_computation.6 | convolution fusion | flops 4837343232 | bytes 12584960 | tf_op jit(solution)/shard_map/dot_general | solution.py:16
  19.0 6.7 %copy.24 = bf16[3072,768]{1,0:T(8,128)(2,1)} copy(bf16[3072,768]{0,1:T(8,128)(2,1)} %fusion.2) | data formatting | bytes 9437184 | tf_op jit(solution)/shard_map/convert_element_type | solution.py:69
  25.6 2.7 copy.25
  28.3 9.7 %all_to_all.42 = bf16[16,2,96,768]{3,2,0,1:T(8,128)(2,1)} all-to-all(bf16[16,2,96,768]{3,2,0,1:T(8,128)(2,1)S(1)} %copy.25), channel_id=1, replica_groups=mesh['pairs'=16,'core'=2,'fac'=4] {'core'}, dimensions={1} | all-to-all | bytes 9437184 | tf_op jit(solution)/shard_map/all_to_all | solution.py:47
  38.0 3.5 %reduce_sum.135 = bf16[16,96,768]{2,1,0:T(8,128)(2,1)S(1)} reduce(bf16[16,2,96,768]{3,2,0,1:T(8,128)(2,1)} %all_to_all.42, bf16[]{:T(256)} %constant.44.clone.1), dimensions={1}, to_apply=%region_0.0 | reduce | flops 1179648 | bytes 7077890 | tf_op jit(solution)/shard_map/reduce_sum | solution.py:48
  41.5 43.2 %all_to_all.43 = bf16[16,96,768]{2,1,0:T(8,128)(2,1)S(1)} all-to-all(bf16[16,96,768]{2,1,0:T(8,128)(2,1)S(1)} %reduce_sum.135), channel_id=1, replica_groups=mesh['pairs'=16,'core'=2,'fac'=4] {'pairs'}, dimensions={0} | all-to-all | bytes 4718592 | tf_op jit(solution)/shard_map/all_to_all | solution.py:49
  84.7 0.3 convert_reduce_fusion
  85.1 0.0 all-gather.5.cloned.1.call-done
  85.1 0.7 negate_convert_fusion
  85.8 0.0 all-gather.7.cloned.1.call-update
  85.8 0.0 all-gather.9.cloned.1.call-start
  85.9 6.2 %gather_fusion = f32[1024]{0:T(1024)S(1)} fusion(f32[32768]{0:T(1024)S(1)} %copy-done, s32[1024]{0:T(1024)S(1)} %fusion.19), kind=kCustom, calls=%fused_computation | custom fusion | bytes 12288 | tf_op jit(solution)/shard_map/gather | solution.py:65
  92.1 1.7 multiply_convert_fusion.1
  93.8 1.1 copy-done.2
  95.0 7.0 %fusion.3 = bf16[3072,384]{0,1:T(8,128)(2,1)} fusion(bf16[1024,3072]{1,0:T(8,128)(2,1)} %param.7, bf16[1024,768]{1,0:T(8,128)(2,1)S(1)} %multiply_convert_fusion.1), kind=kOutput, calls=%fused_computation.9 | convolution fusion | flops 2417098752 | bytes 9437184 | tf_op jit(solution)/shard_map/dot_general | solution.py:16
  101.9 3.0 copy.26
  104.9 0.2 copy.27
  105.2 6.1 %all_to_all.44 = bf16[16,2,96,384]{3,2,0,1:T(8,128)(2,1)S(1)} all-to-all(bf16[16,2,96,384]{3,2,0,1:T(8,128)(2,1)S(1)} %copy.27), channel_id=1, replica_groups=mesh['pairs'=16,'core'=2,'fac'=4] {'core'}, dimensions={1} | all-to-all | bytes 4718592 | tf_op jit(solution)/shard_map/all_to_all | solution.py:47
  111.3 1.8 reduce_sum.137
  113.1 30.0 %all_to_all.45 = bf16[16,96,384]{2,1,0:T(8,128)(2,1)S(1)} all-to-all(bf16[16,96,384]{2,1,0:T(8,128)(2,1)} %reduce_sum.137), channel_id=1, replica_groups=mesh['pairs'=16,'core'=2,'fac'=4] {'pairs'}, dimensions={0} | all-to-all | bytes 2359296 | tf_op jit(solution)/shard_map/all_to_all | solution.py:49
  143.1 0.2 convert_reduce_fusion.2
  143.2 2.0 all-gather.7.cloned.1.call-done
  145.3 3.2 fusion.15
  148.5 11.5 %all_gather.23 = bf16[96,3072]{1,0:T(8,128)(2,1)S(1)} all-gather(bf16[96,768]{1,0:T(8,128)(2,1)S(1)} %fusion.15), channel_id=1, replica_groups=mesh['pairs'=16,'core'=2,'fac'=4] {'fac'}, dimensions={1}, use_global_device_ids=true | all-gather | bytes 737280 | tf_op jit(solution)/shard_map/all_gather | solution.py:79
  160.0 3.9 %fusion.27 = (bf16[96,768]{1,0:T(8,128)(2,1)}, f32[96,768]{1,0:T(8,128)S(1)}) fusion(bf16[96,3072]{1,0:T(8,128)(2,1)S(1)} %all_gather.23, bf16[3072,768]{1,0:T(8,128)(2,1)} %param.13), kind=kOutput, calls=%fused_computation.59 | convolution fusion | flops 453058560 | bytes 5750784 | tf_op jit(solution)/shard_map/dot_general | solution.py:78
  163.9 0.0 all-gather.11.cloned.1.call-start
  163.9 6.8 %fusion.4 = bf16[3072,384]{0,1:T(8,128)(2,1)} fusion(bf16[1024,3072]{1,0:T(8,128)(2,1)} %param.7, bf16[1024,768]{1,0:T(8,128)(2,1)S(1)} %copy-done.3), kind=kOutput, calls=%fused_computation.10 | convolution fusion | flops 2417098752 | bytes 9437184 | tf_op jit(solution)/shard_map/dot_general | solution.py:16
  170.8 3.0 copy.28
  173.8 0.2 copy.29
  174.0 7.5 %all_to_all.46 = bf16[16,2,96,384]{3,2,0,1:T(8,128)(2,1)S(1)} all-to-all(bf16[16,2,96,384]{3,2,0,1:T(8,128)(2,1)S(1)} %copy.29), channel_id=1, replica_groups=mesh['pairs'=16,'core'=2,'fac'=4] {'core'}, dimensions={1} | all-to-all | bytes 4718592 | tf_op jit(solution)/shard_map/all_to_all | solution.py:47
  181.5 1.8 reduce_sum.140
  183.3 26.3 %all_to_all.47 = bf16[16,96,384]{2,1,0:T(8,128)(2,1)S(1)} all-to-all(bf16[16,96,384]{2,1,0:T(8,128)(2,1)} %reduce_sum.140), channel_id=1, replica_groups=mesh['pairs'=16,'core'=2,'fac'=4] {'pairs'}, dimensions={0} | all-to-all | bytes 2359296 | tf_op jit(solution)/shard_map/all_to_all | solution.py:49
  209.6 0.2 convert_reduce_fusion.1
  209.8 11.7 %all_gather.24 = bf16[96,3072]{1,0:T(8,128)(2,1)S(1)} all-gather(bf16[96,768]{1,0:T(8,128)(2,1)S(1)} %pad_maximum_fusion), channel_id=1, replica_groups=mesh['pairs'=16,'core'=2,'fac'=4] {'fac'}, dimensions={1}, use_global_device_ids=true | all-gather | bytes 737280 | tf_op jit(solution)/shard_map/all_gather | solution.py:110
  221.5 4.5 %multiply_reduce_fusion.5 = (f32[]{:T(128)}, f32[]{:T(128)}, bf16[96,768]{1,0:T(8,128)(2,1)}, f32[96,768]{1,0:T(8,128)S(1)}) fusion(f32[96,768]{1,0:T(8,128)S(1)} %get-tuple-element.26, f32[96,768]{1,0:T(8,128)S(1)} %convert_reduce_fusion, bf16[96,3072]{1,0:T(8,128)(2,1)S(1)} %all_gather.24, bf16[3072,768]{1,0:T(8,128)(2,1)} %all-gather.9.cloned.1.call-done), kind=kOutput, calls=%fused_computation.43 | convolution fusion | flops 453574656 | bytes 6340616 | tf_op jit(solution)/shard_map/dot_general | solution.py:12
  226.0 0.0 all-gather.11.cloned.1.call-update
  226.0 3.3 convolution_convert_fusion.3
  229.3 1.4 pad_maximum_fusion.1
  230.6 0.7 broadcast_in_dim.7
  231.3 10.9 %all-to-all-start.6 = ((f32[128,1,2]{2,1,0:T(1,128)}), f32[128,1,2]{2,1,0:T(1,128)S(1)}, u32[]{:S(2)}, u32[]{:S(2)}) async-start(f32[128,1,2]{2,1,0:T(1,128)} %broadcast_in_dim.7), calls=%async_computation.6 | async-start | bytes 131072 | tf_op jit(solution)/shard_map/all_to_all | solution.py:56
  242.2 11.3 %all_gather.26 = bf16[96,3072]{1,0:T(8,128)(2,1)S(1)} all-gather(bf16[96,768]{1,0:T(8,128)(2,1)S(1)} %convolution_convert_fusion.3), channel_id=1, replica_groups=mesh['pairs'=16,'core'=2,'fac'=4] {'fac'}, dimensions={1}, use_global_device_ids=true | all-gather | bytes 737280 | tf_op jit(solution)/shard_map/all_gather | solution.py:119
  253.5 0.2 reduce_sum.143
  253.7 0.6 fusion.26
  255.7 20.6 %all-gather.11.cloned.1.call-done = bf16[3072,768]{1,0:T(8,128)(2,1)} async-done(((bf16[96,768]{1,0:T(8,128)(2,1)}), bf16[3072,768]{1,0:T(8,128)(2,1)}) %all-gather.11.cloned.1.call-update) | async-done | bytes 4718608 | tf_op jit(solution)/shard_map/all_gather | solution.py:73
  276.2 5.6 %fusion.6 = bf16[192,768]{1,0:T(8,128)(2,1)S(1)} fusion(bf16[3072,768]{1,0:T(8,128)(2,1)} %all-gather.11.cloned.1.call-done, bf16[3072,768]{1,0:T(8,128)(2,1)} %all-gather.7.cloned.1.call-done, f32[]{:T(128)S(6)} %div.17, bf16[96,3072]{1,0:T(8,128)(2,1)S(1)} %all_gather.26, bf16[96,3072]{1,0:T(8,128)(2,1)S(1)} %copy-done.5), kind=kOutput, calls=%fused_computation.18 | convolution fusion | flops 920272896 | bytes 10911748 | tf_op jit(solution)/shard_map/dot_general | solution.py:12
  281.8 1.3 collective-permute-start
  283.1 1.5 collective-permute-start.1
  284.6 1.7 fusion.13
  286.2 5.2 %collective-permute-done = bf16[192,768]{1,0:T(8,128)(2,1)S(1)} collective-permute-done((bf16[192,768]{1,0:T(8,128)(2,1)S(1)}, bf16[192,768]{1,0:T(8,128)(2,1)S(1)}, u32[]{:S(2)}, u32[]{:S(2)}) %collective-permute-start) | collective-permute-done | bytes 294944 | tf_op jit(solution)/shard_map/ppermute | solution.py:36
  291.4 1.7 convolution_add_fusion.2
  293.2 1.7 convolution_add_fusion.1
  294.9 5.2 %collective-permute-done.2 = bf16[192,768]{1,0:T(8,128)(2,1)S(1)} collective-permute-done((bf16[192,768]{1,0:T(8,128)(2,1)S(1)}, bf16[192,768]{1,0:T(8,128)(2,1)S(1)}, u32[]{:S(2)}, u32[]{:S(2)}) %collective-permute-start.2) | collective-permute-done | bytes 294944 | tf_op jit(solution)/shard_map/ppermute | solution.py:36
  300.1 1.7 convolution_add_fusion
  301.8 0.8 multiply_reduce_fusion.3
  302.6 2.5 pad_maximum_fusion.2
  305.2 16.0 %all_to_all.48 = f32[128,1,4]{2,1,0:T(1,128)S(1)} all-to-all(f32[128,1,4]{2,1,0:T(1,128)S(1)} %broadcast_in_dim.8), channel_id=1, replica_groups=mesh['pairs'=16,'core'=2,'fac'=4] {'pairs','core','fac'}, dimensions={0} | all-to-all | bytes 4096 | tf_op jit(solution)/shard_map/all_to_all | solution.py:56
  321.1 0.2 reduce_sum.148
  321.3 0.6 fusion.25
  326.4 1.0 multiply_subtract_fusion
  (24 shorter events, 0.1 us)
Async XLA Ops:
  7.2 78.7 %copy-start = (f32[32768]{0:T(1024)S(1)}, f32[32768]{0:T(1024)}, u32[]{:S(2)}) copy-start(f32[32768]{0:T(1024)} %param.11) | copy-start | bytes 393220
  7.2 77.9 %all-gather.5.cloned.1.call-start = ((), (), s32[]{:S(2)}) async-start(), calls=%async_computation.8 | async-start | bytes 4866048 | tf_op jit(solution)/shard_map/all_gather | solution.py:88
  8.8 136.4 %all-gather.7.cloned.1.call-start = ((), (), s32[]{:S(2)}) async-start(), calls=%async_computation.9 | async-start | bytes 4866048 | tf_op jit(solution)/shard_map/all_gather | solution.py:73
  41.5 44.3 %copy-start.7 = (s32[1024]{0:T(1024)S(1)}, s32[1024]{0:T(1024)}, u32[]{:S(2)}) copy-start(s32[1024]{0:T(1024)} %param.9) | copy-start | bytes 12292
  84.7 7.3 %copy-start.6 = (s32[1024]{0:T(1024)S(1)}, s32[1024]{0:T(1024)}, u32[]{:S(2)}) copy-start(s32[1024]{0:T(1024)} %param.10) | copy-start | bytes 12292
  85.8 135.7 %all-gather.9.cloned.1.call-start = ((), (), s32[]{:S(2)}) async-start(), calls=%async_computation.10 | async-start | bytes 4866048 | tf_op jit(solution)/shard_map/all_gather | solution.py:73
  93.8 1.1 copy-start.2
  111.3 34.0 %copy-start.4 = (bf16[96,3072]{1,0:T(8,128)(2,1)S(1)}, bf16[96,3072]{1,0:T(8,128)(2,1)}, u32[]{:S(2)}) copy-start(bf16[96,3072]{1,0:T(8,128)(2,1)} %param.12) | copy-start | bytes 1769476
  143.2 20.7 %copy-start.3 = (bf16[1024,768]{1,0:T(8,128)(2,1)S(1)}, bf16[1024,768]{1,0:T(8,128)(2,1)}, u32[]{:S(2)}) copy-start(bf16[1024,768]{1,0:T(8,128)(2,1)} %copy-done.2) | copy-start | bytes 4718596
  163.9 112.4 %all-gather.11.cloned.1.call-start = ((), (), s32[]{:S(2)}) async-start(), calls=%async_computation.11 | async-start | bytes 4866048 | tf_op jit(solution)/shard_map/all_gather | solution.py:73
  226.0 50.3 %copy-start.5 = (bf16[96,3072]{1,0:T(8,128)(2,1)S(1)}, bf16[96,3072]{1,0:T(8,128)(2,1)}, u32[]{:S(2)}) copy-start(bf16[96,3072]{1,0:T(8,128)(2,1)} %param.12) | copy-start | bytes 1769476
  231.3 22.2 %all-to-all-start.6 = ((f32[128,1,2]{2,1,0:T(1,128)}), f32[128,1,2]{2,1,0:T(1,128)S(1)}, u32[]{:S(2)}, u32[]{:S(2)}) async-start(f32[128,1,2]{2,1,0:T(1,128)} %broadcast_in_dim.7), calls=%async_computation.6 | async-start | bytes 131072 | tf_op jit(solution)/shard_map/all_to_all | solution.py:56
  281.8 9.6 %collective-permute-start = (bf16[192,768]{1,0:T(8,128)(2,1)S(1)}, bf16[192,768]{1,0:T(8,128)(2,1)S(1)}, u32[]{:S(2)}, u32[]{:S(2)}) collective-permute-start(bf16[192,768]{1,0:T(8,128)(2,1)S(1)} %fusion.6), channel_id=1, source_target_pairs={{0,1},{1,2},{2,3},{3,0},{4,5},{5,6},{6,7},{7,4},{8,9},{9,10},{10,1... | collective-permute-start | bytes 884744 | tf_op jit(solution)/shard_map/ppermute | solution.py:36
  283.1 10.1 %collective-permute-start.1 = (bf16[192,768]{1,0:T(8,128)(2,1)S(1)}, bf16[192,768]{1,0:T(8,128)(2,1)S(1)}, u32[]{:S(2)}, u32[]{:S(2)}) collective-permute-start(bf16[192,768]{1,0:T(8,128)(2,1)S(1)} %fusion.6), channel_id=1, source_target_pairs={{0,3},{1,0},{2,1},{3,2},{4,7},{5,4},{6,5},{7,6},{8,11},{9,8},{10,9... | collective-permute-start | bytes 884744 | tf_op jit(solution)/shard_map/ppermute | solution.py:39
  291.4 8.6 %collective-permute-start.2 = (bf16[192,768]{1,0:T(8,128)(2,1)S(1)}, bf16[192,768]{1,0:T(8,128)(2,1)S(1)}, u32[]{:S(2)}, u32[]{:S(2)}) collective-permute-start(bf16[192,768]{1,0:T(8,128)(2,1)S(1)} %collective-permute-done), channel_id=1, source_target_pairs={{0,1},{1,2},{2,3},{3,0},{4,5},{5,6},{6,7},{7,4},{8,9},{9,10},{10,1... | collective-permute-start | bytes 884744 | tf_op jit(solution)/shard_map/ppermute | solution.py:36
  291.4 35.9 %copy-start.1 = (f32[32768]{0:T(1024)S(1)}, f32[32768]{0:T(1024)}, u32[]{:S(2)}) copy-start(f32[32768]{0:T(1024)} %param.11) | copy-start | bytes 393220
Sparse Core Ops, SparseCore 0:
  10.8 68.8 all-gather.4
  85.9 59.2 all-gather.6
  164.0 53.3 all-gather.8
  226.1 50.0 all-gather.10
where the time goes:
time: 335 us; the launch traced here: 334 us
  blocking collectives  173 us (52%)
  matrix products  50.4 us (15%)
  waiting for transfers between devices  33.1 us (10%)
  local copies, waits for them, and re-layouts  26.6 us (8%)
  between operations  19.9 us (6%)
  other arithmetic  16.8 us (5%)
  starting transfers between devices  13.8 us (4%)
    all_to_all x3, blocking collectives, scatter_sum(): received = lax.all_to_all(chip_sum, 'pairs', 0, 0, tiled=False)  99.5 us
    all_to_all x3, blocking collectives, scatter_sum(): on_chip = lax.all_to_all(blocks, 'core', 1, 1, tiled=False)  23.4 us
    dot_general x8, matrix products, add_columns(): return jnp.dot(matrix, piece, preferred_element_type=jnp.float32)  23.3 us
    dot_general x3, matrix products, transposed_term(): lax.dot_general(matrix, right, (((0,), (0,)), ((), ())), preferred_elemen...  23.2 us
    all_gather x3, waiting for transfers between devices, gather_rows(): return lax.all_gather(matrix.astype(jnp.bfloat16), FSDP, axis=0, tiled=True)  22.6 us
    all_to_all x1, blocking collectives, global_sums(): received = lax.all_to_all(stacked, FSDP + ('fac',), 0, 0, tiled=True)  16 us
    all_gather x1, blocking collectives, body(): lax.all_gather(gram_own.astype(jnp.bfloat16), 'fac', axis=1, tiled=True)  11.7 us
    all_gather x1, blocking collectives, precondition(): lax.all_gather(mixed_low, 'fac', axis=1, tiled=True)  11.5 us
  transfers between devices with their start and end apart: 8, of which 4 were waited for; matrix products, arithmetic and copies ran while one was open for 20% of the time, Pallas kernels for 0%

commit v1 on v0

--- a/solution.py
+++ b/solution.py
@@ -1,3 +1,4 @@
+import functools
 import math
 import jax
 import jax.numpy as jnp
@@ -6,6 +7,17 @@
 
 ITERS = 2
 damping = 0.3
+
+
+def refer_sheets(panel, which_axis, which_dim):
+    all_rows = jnp.concatenate([panel for _ in range(lax.axis_size(which_axis))], axis=which_dim)
+    current_block = lax.all_to_all(
+        all_rows, which_axis, split_axis=which_dim, concat_axis=which_dim, tiled=True
+    )
+    return current_block
+
+
+do_local_data = functools.partial(refer_sheets, which_axis="fac", which_dim=1)
 
 
 def add_columns(matrix, piece):
@@ -116,9 +128,7 @@
     image = curvature(direction)
     image_rows = gather_rows(image)
     inner_now, energy = global_sums(inner_part(residual, precond), inner_part(direction, image))
-    gram_inverse = lax.all_gather(
-        add_columns(gram_rows, in_cols).astype(jnp.bfloat16), "fac", axis=1, tiled=True
-    )
+    gram_inverse = do_local_data(add_columns(gram_rows, in_cols).astype(jnp.bfloat16))
     alpha = inner_now / energy
     newton_step = alpha * direction
     residual = residual - alpha * image

time: 335 us -> 336 us (level)
  blocking collectives: 173 us -> 162 us
  waiting for transfers between devices: 33.1 us -> 40 us
  starting transfers between devices: 13.8 us -> 17.4 us
    all_gather x1 -> x0, blocking collectives: 11.3 us -> none  [body(): lax.all_gather(add_columns(gram_rows, in_cols).astype(jnp.bfloat16), 'fac...]
    all_to_all x1, waiting for transfers between devices: 0.01 us -> 9.58 us  [global_sums(): received = lax.all_to_all(stacked, FSDP + ('fac',), 0, 0, tiled=True)]
    all_gather x3, waiting for transfers between devices: 22.6 us -> 13.9 us  [gather_rows(): return lax.all_gather(matrix.astype(jnp.bfloat16), FSDP, axis=0, tiled=True)]
    all_to_all x0 -> x1, waiting for transfers between devices: none -> 5.93 us  [refer_sheets(): lax.all_to_all(all_rows, which_axis, split_axis=which_dim, concat_axis=wh...]
    all_to_all x0 -> x1, starting transfers between devices: none -> 4.67 us  [refer_sheets(): lax.all_to_all(all_rows, which_axis, split_axis=which_dim, concat_axis=wh...]
  transfers between devices with their start and end apart: 8 -> 9, of which waited for: 4 -> 6; matrix products, arithmetic and copies ran while one was open for 20% -> 20% of each run, Pallas kernels for 0% -> 0%
where the time goes in v1:
time: 336 us; the launch traced here: 334 us
  blocking collectives  162 us (48%)
  matrix products  50.3 us (15%)
  waiting for transfers between devices  40 us (12%)
  local copies, waits for them, and re-layouts  27.5 us (8%)
  between operations  19.9 us (6%)
  starting transfers between devices  17.4 us (5%)
  other arithmetic  16.8 us (5%)
    all_to_all x3, blocking collectives, scatter_sum(): received = lax.all_to_all(chip_sum, 'pairs', 0, 0, tiled=False)  99.5 us
    all_to_all x3, blocking collectives, scatter_sum(): on_chip = lax.all_to_all(blocks, 'core', 1, 1, tiled=False)  23.4 us
    dot_general x8, matrix products, add_columns(): return jnp.dot(matrix, piece, preferred_element_type=jnp.float32)  23.2 us
    dot_general x3, matrix products, transposed_term(): lax.dot_general(matrix, right, (((0,), (0,)), ((), ())), preferred_elemen...  23.2 us
    all_to_all x1, blocking collectives, global_sums(): received = lax.all_to_all(stacked, FSDP + ('fac',), 0, 0, tiled=True)  15.9 us
    all_gather x3, waiting for transfers between devices, gather_rows(): return lax.all_gather(matrix.astype(jnp.bfloat16), FSDP, axis=0, tiled=True)  13.9 us
    all_gather x1, blocking collectives, body(): lax.all_gather(gram_own.astype(jnp.bfloat16), 'fac', axis=1, tiled=True)  11.7 us
    all_gather x1, blocking collectives, precondition(): lax.all_gather(mixed_low, 'fac', axis=1, tiled=True)  11.6 us
  transfers between devices with their start and end apart: 9, of which 6 were waited for; matrix products, arithmetic and copies ran while one was open for 20% of the time, Pallas kernels for 0%

profile of v1, /device:TPU:1, one launch (start us, length us, event | category | flops | bytes accessed | tf_op | source)
XLA Modules:
  0.0 334.0 jit_solution(7161897839390418423)
XLA Ops:
  7.2 0.0 all-gather.5.cloned.1.call-start
  7.2 1.6 constant_dynamic-slice_fusion
  8.8 0.0 all-gather.7.cloned.1.call-start
  8.9 0.7 convert_element_type.76
  9.6 9.4 %fusion.2 = bf16[3072,768]{0,1:T(8,128)(2,1)} fusion(bf16[1024,3072]{1,0:T(8,128)(2,1)} %param.7, bf16[1024,768]{1,0:T(8,128)(2,1)} %param.8, bf16[1024]{0:T(1024)(128)(2,1)S(1)} %convert_element_type.76), kind=kOutput, calls=%fused_computation.6 | convolution fusion | flops 4837343232 | bytes 12584960 | tf_op jit(solution)/shard_map/dot_general | solution.py:28
  19.0 6.7 %copy.35 = bf16[3072,768]{1,0:T(8,128)(2,1)} copy(bf16[3072,768]{0,1:T(8,128)(2,1)} %fusion.2) | data formatting | bytes 9437184 | tf_op jit(solution)/shard_map/convert_element_type | solution.py:81
  25.6 2.7 copy.36
  28.3 9.7 %all_to_all.54 = bf16[16,2,96,768]{3,2,0,1:T(8,128)(2,1)} all-to-all(bf16[16,2,96,768]{3,2,0,1:T(8,128)(2,1)S(1)} %copy.36), channel_id=1, replica_groups=mesh['pairs'=16,'core'=2,'fac'=4] {'core'}, dimensions={1} | all-to-all | bytes 9437184 | tf_op jit(solution)/shard_map/all_to_all | solution.py:59
  38.0 3.5 %reduce_sum.135 = bf16[16,96,768]{2,1,0:T(8,128)(2,1)S(1)} reduce(bf16[16,2,96,768]{3,2,0,1:T(8,128)(2,1)} %all_to_all.54, bf16[]{:T(256)} %constant.44.clone.1), dimensions={1}, to_apply=%region_0.0 | reduce | flops 1179648 | bytes 7077890 | tf_op jit(solution)/shard_map/reduce_sum | solution.py:60
  41.5 43.2 %all_to_all.55 = bf16[16,96,768]{2,1,0:T(8,128)(2,1)S(1)} all-to-all(bf16[16,96,768]{2,1,0:T(8,128)(2,1)S(1)} %reduce_sum.135), channel_id=1, replica_groups=mesh['pairs'=16,'core'=2,'fac'=4] {'pairs'}, dimensions={0} | all-to-all | bytes 4718592 | tf_op jit(solution)/shard_map/all_to_all | solution.py:61
  84.7 0.3 convert_reduce_fusion
  85.1 0.7 negate_convert_fusion
  85.8 0.0 all-gather.9.cloned.1.call-start
  85.9 6.2 %gather_fusion = f32[1024]{0:T(1024)S(1)} fusion(f32[32768]{0:T(1024)S(1)} %copy-done, s32[1024]{0:T(1024)S(1)} %fusion.19), kind=kCustom, calls=%fused_computation | custom fusion | bytes 12288 | tf_op jit(solution)/shard_map/gather | solution.py:77
  92.1 1.7 multiply_convert_fusion.1
  93.8 1.1 copy-done.2
  95.0 7.0 %fusion.3 = bf16[3072,384]{0,1:T(8,128)(2,1)} fusion(bf16[1024,3072]{1,0:T(8,128)(2,1)} %param.7, bf16[1024,768]{1,0:T(8,128)(2,1)S(1)} %multiply_convert_fusion.1), kind=kOutput, calls=%fused_computation.9 | convolution fusion | flops 2417098752 | bytes 9437184 | tf_op jit(solution)/shard_map/dot_general | solution.py:28
  101.9 3.0 copy.37
  104.9 0.2 copy.38
  105.2 6.1 %all_to_all.56 = bf16[16,2,96,384]{3,2,0,1:T(8,128)(2,1)S(1)} all-to-all(bf16[16,2,96,384]{3,2,0,1:T(8,128)(2,1)S(1)} %copy.38), channel_id=1, replica_groups=mesh['pairs'=16,'core'=2,'fac'=4] {'core'}, dimensions={1} | all-to-all | bytes 4718592 | tf_op jit(solution)/shard_map/all_to_all | solution.py:59
  111.3 1.8 reduce_sum.137
  113.1 30.0 %all_to_all.57 = bf16[16,96,384]{2,1,0:T(8,128)(2,1)S(1)} all-to-all(bf16[16,96,384]{2,1,0:T(8,128)(2,1)} %reduce_sum.137), channel_id=1, replica_groups=mesh['pairs'=16,'core'=2,'fac'=4] {'pairs'}, dimensions={0} | all-to-all | bytes 2359296 | tf_op jit(solution)/shard_map/all_to_all | solution.py:61
  143.1 0.2 convert_reduce_fusion.2
  143.2 2.0 all-gather.7.cloned.1.call-done
  145.3 3.2 fusion.15
  148.5 11.6 %all_gather.20 = bf16[96,3072]{1,0:T(8,128)(2,1)S(1)} all-gather(bf16[96,768]{1,0:T(8,128)(2,1)S(1)} %fusion.15), channel_id=1, replica_groups=mesh['pairs'=16,'core'=2,'fac'=4] {'fac'}, dimensions={1}, use_global_device_ids=true | all-gather | bytes 737280 | tf_op jit(solution)/shard_map/all_gather | solution.py:91
  160.1 3.9 %fusion.27 = (bf16[96,768]{1,0:T(8,128)(2,1)}, f32[96,768]{1,0:T(8,128)S(1)}) fusion(bf16[96,3072]{1,0:T(8,128)(2,1)S(1)} %all_gather.20, bf16[3072,768]{1,0:T(8,128)(2,1)} %param.13), kind=kOutput, calls=%fused_computation.61 | convolution fusion | flops 453058560 | bytes 5750784 | tf_op jit(solution)/shard_map/dot_general | solution.py:90
  164.0 0.0 all-gather.11.cloned.1.call-start
  164.1 6.8 %fusion.4 = bf16[3072,384]{0,1:T(8,128)(2,1)} fusion(bf16[1024,3072]{1,0:T(8,128)(2,1)} %param.7, bf16[1024,768]{1,0:T(8,128)(2,1)S(1)} %copy-done.3), kind=kOutput, calls=%fused_computation.10 | convolution fusion | flops 2417098752 | bytes 9437184 | tf_op jit(solution)/shard_map/dot_general | solution.py:28
  170.9 3.0 copy.39
  173.9 0.2 copy.40
  174.2 7.5 %all_to_all.58 = bf16[16,2,96,384]{3,2,0,1:T(8,128)(2,1)S(1)} all-to-all(bf16[16,2,96,384]{3,2,0,1:T(8,128)(2,1)S(1)} %copy.40), channel_id=1, replica_groups=mesh['pairs'=16,'core'=2,'fac'=4] {'core'}, dimensions={1} | all-to-all | bytes 4718592 | tf_op jit(solution)/shard_map/all_to_all | solution.py:59
  181.7 1.8 reduce_sum.140
  183.5 26.3 %all_to_all.59 = bf16[16,96,384]{2,1,0:T(8,128)(2,1)S(1)} all-to-all(bf16[16,96,384]{2,1,0:T(8,128)(2,1)} %reduce_sum.140), channel_id=1, replica_groups=mesh['pairs'=16,'core'=2,'fac'=4] {'pairs'}, dimensions={0} | all-to-all | bytes 2359296 | tf_op jit(solution)/shard_map/all_to_all | solution.py:61
  209.7 0.2 convert_reduce_fusion.1
  209.9 11.7 %all_gather.21 = bf16[96,3072]{1,0:T(8,128)(2,1)S(1)} all-gather(bf16[96,768]{1,0:T(8,128)(2,1)S(1)} %pad_maximum_fusion.1), channel_id=1, replica_groups=mesh['pairs'=16,'core'=2,'fac'=4] {'fac'}, dimensions={1}, use_global_device_ids=true | all-gather | bytes 737280 | tf_op jit(solution)/shard_map/all_gather | solution.py:122
  221.6 4.5 %multiply_reduce_fusion.5 = (f32[]{:T(128)}, f32[]{:T(128)}, bf16[96,768]{1,0:T(8,128)(2,1)}, f32[96,768]{1,0:T(8,128)S(1)}) fusion(f32[96,768]{1,0:T(8,128)S(1)} %get-tuple-element.26, f32[96,768]{1,0:T(8,128)S(1)} %convert_reduce_fusion, bf16[96,3072]{1,0:T(8,128)(2,1)S(1)} %all_gather.21, bf16[3072,768]{1,0:T(8,128)(2,1)} %all-gather.9.cloned.1.call-done), kind=kOutput, calls=%fused_computation.45 | convolution fusion | flops 453574656 | bytes 6340616 | tf_op jit(solution)/shard_map/dot_general | solution.py:24
  226.2 3.2 convolution_convert_fusion.3
  229.4 0.8 copy.56
  230.3 4.7 %all-to-all-start.7 = ((bf16[96,4,768]{2,0,1:T(8,128)(2,1)}), bf16[96,4,768]{2,0,1:T(8,128)(2,1)S(1)}, u32[]{:S(2)}, u32[]{:S(2)}) async-start(bf16[96,4,768]{2,0,1:T(8,128)(2,1)} %bitcast.42), calls=%async_computation.7 | async-start | bytes 1179648 | tf_op jit(solution)/shard_map/all_to_all | solution.py:14
  235.0 1.4 pad_maximum_fusion.2
  236.3 5.9 %all-to-all-done.7 = bf16[96,4,768]{2,0,1:T(8,128)(2,1)S(1)} async-done(((bf16[96,4,768]{2,0,1:T(8,128)(2,1)}), bf16[96,4,768]{2,0,1:T(8,128)(2,1)S(1)}, u32[]{:S(2)}, u32[]{:S(2)}) %all-to-all-start.7) | async-done | bytes 589856 | tf_op jit(solution)/shard_map/all_to_all | solution.py:14
  242.2 0.7 broadcast_in_dim.7
  242.9 9.8 %all-to-all-start.6 = ((f32[128,1,2]{2,1,0:T(1,128)}), f32[128,1,2]{2,1,0:T(1,128)S(1)}, u32[]{:S(2)}, u32[]{:S(2)}) async-start(f32[128,1,2]{2,1,0:T(1,128)} %broadcast_in_dim.7), calls=%async_computation.6 | async-start | bytes 131072 | tf_op jit(solution)/shard_map/all_to_all | solution.py:68
  252.7 0.1 copy.54
  252.8 9.6 %all-to-all-done.6 = f32[128,1,2]{2,1,0:T(1,128)S(1)} async-done(((f32[128,1,2]{2,1,0:T(1,128)}), f32[128,1,2]{2,1,0:T(1,128)S(1)}, u32[]{:S(2)}, u32[]{:S(2)}) %all-to-all-start.6) | async-done | bytes 1056 | tf_op jit(solution)/shard_map/all_to_all | solution.py:68
  262.4 0.2 reduce_sum.143
  262.5 0.6 fusion.26
  264.5 11.9 %all-gather.11.cloned.1.call-done = bf16[3072,768]{1,0:T(8,128)(2,1)} async-done(((bf16[96,768]{1,0:T(8,128)(2,1)}), bf16[3072,768]{1,0:T(8,128)(2,1)}) %all-gather.11.cloned.1.call-update) | async-done | bytes 4718608 | tf_op jit(solution)/shard_map/all_gather | solution.py:85
  276.4 5.6 %fusion.6 = bf16[192,768]{1,0:T(8,128)(2,1)S(1)} fusion(bf16[3072,768]{1,0:T(8,128)(2,1)} %all-gather.11.cloned.1.call-done, bf16[3072,768]{1,0:T(8,128)(2,1)} %all-gather.7.cloned.1.call-done, f32[]{:T(128)S(6)} %div.17, bf16[96,3072]{1,0:T(8,128)(2,1)S(1)} %bitcast.48, bf16[96,3072]{1,0:T(8,128)(2,1)S(1)} %copy-done.5), kind=kOutput, calls=%fused_computation.18 | convolution fusion | flops 920272896 | bytes 10911748 | tf_op jit(solution)/shard_map/dot_general | solution.py:24
  282.0 1.3 collective-permute-start
  283.2 1.5 collective-permute-start.1
  284.7 1.7 fusion.13
  286.4 5.2 %collective-permute-done = bf16[192,768]{1,0:T(8,128)(2,1)S(1)} collective-permute-done((bf16[192,768]{1,0:T(8,128)(2,1)S(1)}, bf16[192,768]{1,0:T(8,128)(2,1)S(1)}, u32[]{:S(2)}, u32[]{:S(2)}) %collective-permute-start) | collective-permute-done | bytes 294944 | tf_op jit(solution)/shard_map/ppermute | solution.py:48
  291.6 1.7 convolution_add_fusion.2
  293.3 1.7 convolution_add_fusion.1
  295.0 5.2 %collective-permute-done.2 = bf16[192,768]{1,0:T(8,128)(2,1)S(1)} collective-permute-done((bf16[192,768]{1,0:T(8,128)(2,1)S(1)}, bf16[192,768]{1,0:T(8,128)(2,1)S(1)}, u32[]{:S(2)}, u32[]{:S(2)}) %collective-permute-start.2) | collective-permute-done | bytes 294944 | tf_op jit(solution)/shard_map/ppermute | solution.py:48
  300.3 1.7 convolution_add_fusion
  301.9 0.8 multiply_reduce_fusion.3
  302.8 2.5 pad_maximum_fusion.3
  305.4 15.9 %all_to_all.60 = f32[128,1,4]{2,1,0:T(1,128)S(1)} all-to-all(f32[128,1,4]{2,1,0:T(1,128)S(1)} %broadcast_in_dim.8), channel_id=1, replica_groups=mesh['pairs'=16,'core'=2,'fac'=4] {'pairs','core','fac'}, dimensions={0} | all-to-all | bytes 4096 | tf_op jit(solution)/shard_map/all_to_all | solution.py:68
  321.3 0.2 reduce_sum.148
  321.4 0.6 fusion.25
  326.6 1.0 multiply_subtract_fusion
  (28 shorter events, 0.2 us)
Async XLA Ops:
  7.2 78.7 %copy-start = (f32[32768]{0:T(1024)S(1)}, f32[32768]{0:T(1024)}, u32[]{:S(2)}) copy-start(f32[32768]{0:T(1024)} %param.11) | copy-start | bytes 393220
  7.2 77.9 %all-gather.5.cloned.1.call-start = ((), (), s32[]{:S(2)}) async-start(), calls=%async_computation.9 | async-start | bytes 4866048 | tf_op jit(solution)/shard_map/all_gather | solution.py:100
  8.8 136.4 %all-gather.7.cloned.1.call-start = ((), (), s32[]{:S(2)}) async-start(), calls=%async_computation.10 | async-start | bytes 4866048 | tf_op jit(solution)/shard_map/all_gather | solution.py:85
  41.5 44.3 %copy-start.7 = (s32[1024]{0:T(1024)S(1)}, s32[1024]{0:T(1024)}, u32[]{:S(2)}) copy-start(s32[1024]{0:T(1024)} %param.9) | copy-start | bytes 12292
  84.7 7.3 %copy-start.6 = (s32[1024]{0:T(1024)S(1)}, s32[1024]{0:T(1024)}, u32[]{:S(2)}) copy-start(s32[1024]{0:T(1024)} %param.10) | copy-start | bytes 12292
  85.8 135.8 %all-gather.9.cloned.1.call-start = ((), (), s32[]{:S(2)}) async-start(), calls=%async_computation.11 | async-start | bytes 4866048 | tf_op jit(solution)/shard_map/all_gather | solution.py:85
  93.8 1.1 copy-start.2
  111.3 34.0 %copy-start.4 = (bf16[96,3072]{1,0:T(8,128)(2,1)S(1)}, bf16[96,3072]{1,0:T(8,128)(2,1)}, u32[]{:S(2)}) copy-start(bf16[96,3072]{1,0:T(8,128)(2,1)} %param.12) | copy-start | bytes 1769476
  148.5 15.6 %copy-start.3 = (bf16[1024,768]{1,0:T(8,128)(2,1)S(1)}, bf16[1024,768]{1,0:T(8,128)(2,1)}, u32[]{:S(2)}) copy-start(bf16[1024,768]{1,0:T(8,128)(2,1)} %copy-done.2) | copy-start | bytes 4718596
  164.0 112.4 %all-gather.11.cloned.1.call-start = ((), (), s32[]{:S(2)}) async-start(), calls=%async_computation.12 | async-start | bytes 4866048 | tf_op jit(solution)/shard_map/all_gather | solution.py:85
  229.4 47.0 %copy-start.5 = (bf16[96,3072]{1,0:T(8,128)(2,1)S(1)}, bf16[96,3072]{1,0:T(8,128)(2,1)}, u32[]{:S(2)}) copy-start(bf16[96,3072]{1,0:T(8,128)(2,1)} %param.12) | copy-start | bytes 1769476
  230.3 12.0 %all-to-all-start.7 = ((bf16[96,4,768]{2,0,1:T(8,128)(2,1)}), bf16[96,4,768]{2,0,1:T(8,128)(2,1)S(1)}, u32[]{:S(2)}, u32[]{:S(2)}) async-start(bf16[96,4,768]{2,0,1:T(8,128)(2,1)} %bitcast.42), calls=%async_computation.7 | async-start | bytes 1179648 | tf_op jit(solution)/shard_map/all_to_all | solution.py:14
  242.9 19.5 %all-to-all-start.6 = ((f32[128,1,2]{2,1,0:T(1,128)}), f32[128,1,2]{2,1,0:T(1,128)S(1)}, u32[]{:S(2)}, u32[]{:S(2)}) async-start(f32[128,1,2]{2,1,0:T(1,128)} %broadcast_in_dim.7), calls=%async_computation.6 | async-start | bytes 131072 | tf_op jit(solution)/shard_map/all_to_all | solution.py:68
  282.0 9.6 %collective-permute-start = (bf16[192,768]{1,0:T(8,128)(2,1)S(1)}, bf16[192,768]{1,0:T(8,128)(2,1)S(1)}, u32[]{:S(2)}, u32[]{:S(2)}) collective-permute-start(bf16[192,768]{1,0:T(8,128)(2,1)S(1)} %fusion.6), channel_id=1, source_target_pairs={{0,1},{1,2},{2,3},{3,0},{4,5},{5,6},{6,7},{7,4},{8,9},{9,10},{10,1... | collective-permute-start | bytes 884744 | tf_op jit(solution)/shard_map/ppermute | solution.py:48
  283.2 10.1 %collective-permute-start.1 = (bf16[192,768]{1,0:T(8,128)(2,1)S(1)}, bf16[192,768]{1,0:T(8,128)(2,1)S(1)}, u32[]{:S(2)}, u32[]{:S(2)}) collective-permute-start(bf16[192,768]{1,0:T(8,128)(2,1)S(1)} %fusion.6), channel_id=1, source_target_pairs={{0,3},{1,0},{2,1},{3,2},{4,7},{5,4},{6,5},{7,6},{8,11},{9,8},{10,9... | collective-permute-start | bytes 884744 | tf_op jit(solution)/shard_map/ppermute | solution.py:51
  291.6 8.6 %collective-permute-start.2 = (bf16[192,768]{1,0:T(8,128)(2,1)S(1)}, bf16[192,768]{1,0:T(8,128)(2,1)S(1)}, u32[]{:S(2)}, u32[]{:S(2)}) collective-permute-start(bf16[192,768]{1,0:T(8,128)(2,1)S(1)} %collective-permute-done), channel_id=1, source_target_pairs={{0,1},{1,2},{2,3},{3,0},{4,5},{5,6},{6,7},{7,4},{8,9},{9,10},{10,1... | collective-permute-start | bytes 884744 | tf_op jit(solution)/shard_map/ppermute | solution.py:48
  293.3 34.2 %copy-start.1 = (f32[32768]{0:T(1024)S(1)}, f32[32768]{0:T(1024)}, u32[]{:S(2)}) copy-start(f32[32768]{0:T(1024)} %param.11) | copy-start | bytes 393220
Sparse Core Ops, SparseCore 0:
  10.8 68.8 all-gather.4
  85.9 59.2 all-gather.6
  164.1 53.3 all-gather.8
  226.3 50.0 all-gather.10
